TPU v7x, 512 devices: a whole 4x4x16 slice. The times are simulated.
512 devices in a mesh: fsdp: 32 (over x_lo, z), tp: 16 (over x_hi, y, core).
Axes of the slice: x: 4 (x_hi: 2, x_lo: 2; x = x_hi * 2 + x_lo), y: 4, z: 16, core: 2. Of those that a mesh axis runs over, the one named last changes fastest.
Arguments:
- activations: bfloat16 [16384, 4096], P(('fsdp', 'tp')), may hold values from -6 to 6
- norm_gain: float32 [4096], replicated, may hold values from 0.5 to 1.5
- proj_weight: bfloat16 [3, 4096, 4096], P(None, 'fsdp', 'tp'), may hold values from -0.09375 to 0.09375
- short_filter: float32 [256, 7], P('tp'), may hold values from -3 to 3
- segment_ids: int32 [32, 512], P('fsdp'), may hold values from 0 to 7, never falling along the last dimension, each value on 1 to 256 neighbouring positions
- needle_pos: int32 [32, 16], P('fsdp'), may hold values from 0 to 511
- readout: float32 [4096], replicated, may hold values from -6 to 6
Outputs:
- mixer_out: bfloat16 [16384, 4096], P(('fsdp', 'tp'))
- needle_score: float32 [32, 16], P('fsdp')
Inputs may be any that keep to these rules, and one draw needn't show every extreme that they name: segment_ids never fall along a slab; each document covers 1 to 256 positions.
All inputs are finite; a program needn't handle non-finite values.
Results may differ from a plain program's by a relative error of at most 0.0068.
Values may be sent and summed in bfloat16 or wider, within the bound.
No kernel may reach another device: no remote copies, remote signals or barrier semaphores. Data moves between devices by JAX's collectives and lax.ppermute only.
A program may use at most 64 MiB of HBM per device.

v0:
```python
import math
import jax
import jax.numpy as jnp
from jax import lax
from jax.sharding import PartitionSpec as P

EPSILON = 1e-06


def short_conv(gated_prod, tap_table, segments):
    length = gated_prod.shape[0]
    filtered = jnp.zeros(gated_prod.shape, jnp.float32)
    for offset in range(tap_table.shape[1]):
        shifted = jnp.pad(gated_prod, ((offset, 0), (0, 0)))[:length]
        earlier = jnp.pad(segments, (offset, 0), constant_values=-1)[:length]
        same_doc = (earlier == segments).astype(jnp.float32)
        filtered = filtered + shifted * same_doc[:, None] * tap_table[:, offset][None, :]
    return filtered


def local(activations, norm_gain, proj_weight, short_filter, segment_ids, needle_pos, readout):
    model_width = activations.shape[1]
    local_rows = activations.shape[0]
    tp_size = lax.axis_size("tp")
    channels = proj_weight.shape[2]
    weights = lax.all_gather(proj_weight, "fsdp", axis=1, tiled=True)
    values = activations.astype(jnp.float32)
    scaled = lax.rsqrt(jnp.mean(values * values, axis=1, keepdims=True) + EPSILON)
    normed = (values * scaled * norm_gain[None, :]).astype(jnp.bfloat16)
    spread = jnp.broadcast_to(normed[None], (tp_size,) + normed.shape)
    slab_rows = lax.all_to_all(spread, "tp", 0, 0, tiled=False).reshape(
        tp_size * local_rows, model_width
    )
    projected = jnp.einsum("sk,ikc->isc", slab_rows, weights, preferred_element_type=jnp.float32)
    gated_prod = projected[1] * projected[2]
    tap_table = jnp.repeat(short_filter, channels // short_filter.shape[0], axis=0)
    filtered = short_conv(gated_prod, tap_table, segment_ids[0])
    mixed_local = (projected[0] * filtered).astype(jnp.bfloat16)
    device_rank = lax.axis_index("tp")
    positions = needle_pos[0]
    slab_len = tp_size * local_rows
    picker = (positions[:, None] == jnp.arange(slab_len, dtype=jnp.int32)[None, :]).astype(
        jnp.bfloat16
    )
    picked = jnp.dot(picker, mixed_local, preferred_element_type=jnp.float32)
    own_readout = lax.dynamic_slice_in_dim(readout, device_rank * channels, channels, 0)
    partial_sum = jnp.sum(picked * own_readout[None, :], axis=1)
    partials = lax.all_to_all(
        jnp.broadcast_to(partial_sum[None], (tp_size,) + partial_sum.shape), "tp", 0, 0, tiled=False
    )
    needle_score = (jnp.sum(partials, axis=0) / math.sqrt(model_width))[None, :]
    blocks = mixed_local.reshape(tp_size, local_rows, channels)
    gathered = lax.all_to_all(blocks, "tp", 0, 0, tiled=False)
    own_rows = jnp.transpose(gathered, (1, 0, 2)).reshape(local_rows, tp_size * channels)
    return (own_rows, needle_score)


def solution(mesh):
    in_specs = (
        P(("fsdp", "tp"), None),
        P(),
        P(None, "fsdp", "tp"),
        P("tp", None),
        P("fsdp", None),
        P("fsdp", None),
        P(),
    )
    out_specs = (P(("fsdp", "tp"), None), P("fsdp", None))
    return jax.shard_map(local, mesh=mesh, in_specs=in_specs, out_specs=out_specs, check_vma=False)
```

profile of v0, /device:TPU:1, one launch (start us, length us, event | category | flops | bytes accessed | tf_op | source)
XLA Modules:
  0.0 202.9 jit_solution(14651823412645313950)
XLA Ops:
  7.2 0.0 all-gather.2.cloned.1.call-start
  7.2 0.7 all-gather.2.cloned.1.call-update
  7.9 1.1 fusion.21
  9.0 1.1 fusion.23
  10.1 2.6 %broadcast_in_dim.6 = bf16[16,32,4096]{2,1,0:T(8,128)(2,1)} broadcast(bf16[32,4096]{1,0:T(8,128)(2,1)S(1)} %fusion.23), dimensions={1,2} | broadcast | bytes 4456448 | tf_op jit(solution)/shard_map/broadcast_in_dim | solution.py:30
  12.7 0.0 copy-start
  12.7 0.0 copy-start.1
  12.7 11.3 %all-to-all-start = ((bf16[16,32,4096]{2,1,0:T(8,128)(2,1)}), bf16[16,32,4096]{2,1,0:T(8,128)(2,1)}, u32[]{:S(2)}, u32[]{:S(2)}) async-start(bf16[16,32,4096]{2,1,0:T(8,128)(2,1)} %broadcast_in_dim.6), calls=%async_computation | async-start | bytes 8388608 | tf_op jit(solution)/shard_map/all_to_all | solution.py:31
  24.0 0.0 copy-done
  24.0 0.1 broadcast_in_dim.7
  24.0 0.1 reshape.58
  24.1 0.8 dynamic_slice.3
  24.9 0.0 copy-done.1
  24.9 0.1 fusion.37
  25.0 98.3 %all-to-all-done = bf16[16,32,4096]{2,1,0:T(8,128)(2,1)} async-done(((bf16[16,32,4096]{2,1,0:T(8,128)(2,1)}), bf16[16,32,4096]{2,1,0:T(8,128)(2,1)}, u32[]{:S(2)}, u32[]{:S(2)}) %all-to-all-start) | async-done | bytes 4194336 | tf_op jit(solution)/shard_map/all_to_all | solution.py:31
  123.3 18.9 %all-gather.2.cloned.1.call-done = bf16[3,4096,256]{2,1,0:T(8,128)(2,1)} async-done(((bf16[3,128,256]{2,1,0:T(8,128)(2,1)}), bf16[3,4096,256]{2,1,0:T(8,128)(2,1)}) %all-gather.2.cloned.1.call-update) | async-done | bytes 6291472 | tf_op jit(solution)/shard_map/all_gather | solution.py:26
  142.2 0.0 copy-start.2
  142.2 7.0 %convolution_bitcast_fusion = f32[3,512,256]{2,1,0:T(8,128)S(1)} fusion(bf16[512,4096,1]{1,0,2:T(8,128)(2,1)} %bitcast.1, bf16[3,4096,256]{2,1,0:T(8,128)(2,1)} %all-gather.2.cloned.1.call-done), kind=kOutput, calls=%fused_computation | convolution fusion | flops 3221225472 | bytes 12058624 | tf_op jit(solution)/shard_map/sk,ikc->isc/dot_general | solution.py:34
  149.2 0.1 fusion.24
  149.3 1.5 fusion.10
  150.8 0.0 copy-done.2
  150.8 1.2 fusion
  152.0 30.6 %all_to_all.16 = f32[16,1,16]{2,1,0:T(1,128)S(1)} all-to-all(f32[16,1,16]{2,1,0:T(1,128)S(1)} %broadcast_in_dim.8), channel_id=1, replica_groups=mesh['fsdp'=32,'tp'=16] {'tp'}, dimensions={0} | all-to-all | bytes 2048 | tf_op jit(solution)/shard_map/all_to_all | solution.py:48
  182.6 4.0 %all-to-all-start.1 = ((bf16[16,32,256]{2,1,0:T(8,128)(2,1)}), bf16[16,32,256]{2,1,0:T(8,128)(2,1)S(1)}, u32[]{:S(2)}, u32[]{:S(2)}) async-start(bf16[16,32,256]{2,1,0:T(8,128)(2,1)} %bitcast.13), calls=%async_computation.1 | async-start | bytes 524288 | tf_op jit(solution)/shard_map/all_to_all | solution.py:53
  186.7 0.5 multiply_bitcast_fusion
  187.2 8.2 %all-to-all-done.1 = bf16[16,32,256]{2,1,0:T(8,128)(2,1)S(1)} async-done(((bf16[16,32,256]{2,1,0:T(8,128)(2,1)}), bf16[16,32,256]{2,1,0:T(8,128)(2,1)S(1)}, u32[]{:S(2)}, u32[]{:S(2)}) %all-to-all-start.1) | async-done | bytes 262176 | tf_op jit(solution)/shard_map/all_to_all | solution.py:53
  195.4 0.7 copy.15
  (4 shorter events, 0.0 us)
Async XLA Ops:
  7.2 135.0 %all-gather.2.cloned.1.call-start = ((), (), s32[]{:S(2)}) async-start(), calls=%async_computation.3 | async-start | bytes 6488064 | tf_op jit(solution)/shard_map/all_gather | solution.py:26
  12.7 11.3 %copy-start = (f32[16,7]{0,1:T(8,128)S(1)}, f32[16,7]{0,1:T(8,128)}, u32[]{:S(2)}) copy-start(f32[16,7]{0,1:T(8,128)} %param.10) | copy-start | bytes 1348
  12.7 12.2 %copy-start.1 = (s32[1,512]{1,0:T(1,128)S(1)}, s32[1,512]{1,0:T(1,128)}, u32[]{:S(2)}) copy-start(s32[1,512]{1,0:T(1,128)} %param.11) | copy-start | bytes 6148
  12.7 110.6 %all-to-all-start = ((bf16[16,32,4096]{2,1,0:T(8,128)(2,1)}), bf16[16,32,4096]{2,1,0:T(8,128)(2,1)}, u32[]{:S(2)}, u32[]{:S(2)}) async-start(bf16[16,32,4096]{2,1,0:T(8,128)(2,1)} %broadcast_in_dim.6), calls=%async_computation | async-start | bytes 8388608 | tf_op jit(solution)/shard_map/all_to_all | solution.py:31
  142.2 8.6 %copy-start.2 = (s32[1,16]{1,0:T(1,128)S(1)}, s32[1,16]{1,0:T(1,128)}, u32[]{:S(2)}) copy-start(s32[1,16]{1,0:T(1,128)} %param.12) | copy-start | bytes 196
  182.6 12.7 %all-to-all-start.1 = ((bf16[16,32,256]{2,1,0:T(8,128)(2,1)}), bf16[16,32,256]{2,1,0:T(8,128)(2,1)S(1)}, u32[]{:S(2)}, u32[]{:S(2)}) async-start(bf16[16,32,256]{2,1,0:T(8,128)(2,1)} %bitcast.13), calls=%async_computation.1 | async-start | bytes 524288 | tf_op jit(solution)/shard_map/all_to_all | solution.py:53
Sparse Core Ops, SparseCore 0:
  10.1 132.0 all-gather.1
where the time goes:
time: 203 us
  waiting for transfers between devices  126 us (62%)
  blocking collectives  30.6 us (15%)
  starting transfers between devices  15.3 us (8%)
  between operations  14.1 us (7%)
  matrix products  8.29 us (4%)
  other arithmetic  4.34 us (2%)
  local copies, waits for them, and re-layouts  4.24 us (2%)
    all_to_all x1, waiting for transfers between devices, local(): lax.all_to_all(spread, 'tp', 0, 0, tiled=False)  98.3 us
    all_to_all x1, blocking collectives, local(): lax.all_to_all(jnp.broadcast_to(partial_sum[None], (tp_size,) + partial_s...  30.6 us
    all_gather x1, waiting for transfers between devices, local(): weights = lax.all_gather(proj_weight, 'fsdp', axis=1, tiled=True)  18.9 us
    all_to_all x1, starting transfers between devices, local(): lax.all_to_all(spread, 'tp', 0, 0, tiled=False)  11.3 us
    all_to_all x1, waiting for transfers between devices, local(): gathered = lax.all_to_all(blocks, 'tp', 0, 0, tiled=False)  8.21 us
    dot_general x1, matrix products, local(): jnp.einsum('sk,ikc->isc', slab_rows, weights, preferred_element_type=jnp....  7.04 us
  transfers between devices with their start and end apart: 3, of which 3 were waited for; matrix products, arithmetic and copies ran while one was open for 3% of the time, Pallas kernels for 0%

commit v1 on v0

--- a/solution.py
+++ b/solution.py
@@ -5,6 +5,11 @@
 from jax.sharding import PartitionSpec as P
 
 EPSILON = 1e-06
+
+
+def swapped_in(array, axis, dim):
+    sent = jnp.stack([array] * lax.axis_size(axis))
+    return jnp.concatenate(lax.all_to_all(sent, axis, 0, 0), axis=dim)
 
 
 def short_conv(gated_prod, tap_table, segments):
@@ -23,7 +28,7 @@
     local_rows = activations.shape[0]
     tp_size = lax.axis_size("tp")
     channels = proj_weight.shape[2]
-    weights = lax.all_gather(proj_weight, "fsdp", axis=1, tiled=True)
+    weights = swapped_in(proj_weight, "fsdp", 1)
     values = activations.astype(jnp.float32)
     scaled = lax.rsqrt(jnp.mean(values * values, axis=1, keepdims=True) + EPSILON)
     normed = (values * scaled * norm_gain[None, :]).astype(jnp.bfloat16)

time: 203 us -> 409 us (2.01)
  waiting for transfers between devices: 126 us -> 329 us
  starting transfers between devices: 15.3 us -> 29.8 us
  between operations: 14.1 us -> 0.71 us
  blocking collectives: 30.6 us -> 19.9 us
  local copies, waits for them, and re-layouts: 4.24 us -> 14.7 us
    all_to_all x0 -> x1, waiting for transfers between devices: none -> 273 us  [swapped_in(): return jnp.concatenate(lax.all_to_all(sent, axis, 0, 0), axis=dim)]
    all_to_all x1, waiting for transfers between devices: 98.3 us -> 47.8 us  [local(): lax.all_to_all(spread, 'tp', 0, 0, tiled=False)]
    all_gather x1 -> x0, waiting for transfers between devices: 18.9 us -> none  [local(): weights = lax.all_gather(proj_weight, 'fsdp', axis=1, tiled=True)]
    all_to_all x0 -> x1, starting transfers between devices: none -> 17.2 us  [swapped_in(): return jnp.concatenate(lax.all_to_all(sent, axis, 0, 0), axis=dim)]
    all_to_all x1, blocking collectives: 30.6 us -> 19.9 us  [local(): lax.all_to_all(jnp.broadcast_to(partial_sum[None], (tp_size,) + partial_s...]
    reshape x0 -> x1, local copies, waits for them, and re-layouts: none -> 6.23 us  [swapped_in(): return jnp.concatenate(lax.all_to_all(sent, axis, 0, 0), axis=dim)]
    another operation x0 -> x1, local copies, waits for them, and re-layouts: none -> 4.35 us  [swapped_in(): sent = jnp.stack([array] * lax.axis_size(axis))]
  transfers between devices with their start and end apart: 3 -> 3, of which waited for: 3 -> 3; matrix products, arithmetic and copies ran while one was open for 3% -> 2% of each run, Pallas kernels for 0% -> 0%
where the time goes in v1:
time: 409 us; the launch traced here: 405 us
  waiting for transfers between devices  329 us (80%)
  starting transfers between devices  29.8 us (7%)
  blocking collectives  19.9 us (5%)
  local copies, waits for them, and re-layouts  14.7 us (4%)
  matrix products  8.29 us (2%)
    all_to_all x1, waiting for transfers between devices, swapped_in(): return jnp.concatenate(lax.all_to_all(sent, axis, 0, 0), axis=dim)  273 us
    all_to_all x1, waiting for transfers between devices, local(): lax.all_to_all(spread, 'tp', 0, 0, tiled=False)  47.8 us
    all_to_all x1, blocking collectives, local(): lax.all_to_all(jnp.broadcast_to(partial_sum[None], (tp_size,) + partial_s...  19.9 us
    all_to_all x1, starting transfers between devices, swapped_in(): return jnp.concatenate(lax.all_to_all(sent, axis, 0, 0), axis=dim)  17.2 us
    all_to_all x1, starting transfers between devices, local(): lax.all_to_all(spread, 'tp', 0, 0, tiled=False)  8.63 us
    all_to_all x1, waiting for transfers between devices, local(): gathered = lax.all_to_all(blocks, 'tp', 0, 0, tiled=False)  8.21 us
  transfers between devices with their start and end apart: 3, of which 3 were waited for; matrix products, arithmetic and copies ran while one was open for 2% of the time, Pallas kernels for 0%

profile of v1, /device:TPU:1, one launch (start us, length us, event | category | flops | bytes accessed | tf_op | source)
XLA Modules:
  0.0 405.3 jit_solution(5948755221245836471)
XLA Ops:
  0.6 4.4 %stack.2 = bf16[32,3,128,256]{3,2,1,0:T(8,128)(2,1)} broadcast(bf16[3,128,256]{2,1,0:T(8,128)(2,1)} %param.9), dimensions={1,2,3} | broadcast | bytes 6488064 | tf_op jit(solution)/shard_map/stack | solution.py:11
  5.0 0.0 copy-start
  5.0 0.0 copy-start.1
  5.0 17.2 %all-to-all-start.1 = ((bf16[32,3,128,256]{3,2,1,0:T(8,128)(2,1)}), bf16[32,3,128,256]{3,2,1,0:T(8,128)(2,1)}, u32[]{:S(2)}, u32[]{:S(2)}) async-start(bf16[32,3,128,256]{3,2,1,0:T(8,128)(2,1)} %stack.2), calls=%async_computation.1 | async-start | bytes 12582912 | tf_op jit(solution)/shard_map/all_to_all | solution.py:12
  22.2 0.0 copy-done
  22.2 0.2 fusion.21
  22.4 0.0 copy-done.1
  22.4 0.1 fusion.23
  22.5 273.4 %all-to-all-done.1 = bf16[32,3,128,256]{3,2,1,0:T(8,128)(2,1)} async-done(((bf16[32,3,128,256]{3,2,1,0:T(8,128)(2,1)}), bf16[32,3,128,256]{3,2,1,0:T(8,128)(2,1)}, u32[]{:S(2)}, u32[]{:S(2)}) %all-to-all-start.1) | async-done | bytes 6291488 | tf_op jit(solution)/shard_map/all_to_all | solution.py:12
  295.9 2.4 broadcast_in_dim.6
  298.3 0.0 copy-start.2
  298.3 0.0 copy-start.3
  298.3 8.6 %all-to-all-start = ((bf16[16,32,4096]{2,1,0:T(8,128)(2,1)}), bf16[16,32,4096]{2,1,0:T(8,128)(2,1)}, u32[]{:S(2)}, u32[]{:S(2)}) async-start(bf16[16,32,4096]{2,1,0:T(8,128)(2,1)} %broadcast_in_dim.6), calls=%async_computation | async-start | bytes 8388608 | tf_op jit(solution)/shard_map/all_to_all | solution.py:36
  307.0 0.0 copy-done.2
  307.0 0.1 broadcast_in_dim.7
  307.0 0.1 reshape.68
  307.1 0.8 dynamic_slice.3
  307.9 0.0 copy-done.3
  307.9 0.1 fusion.37
  308.0 6.2 %copy.16 = bf16[3,32,128,256]{3,2,1,0:T(8,128)(2,1)} copy(bf16[3,32,128,256]{3,2,0,1:T(8,128)(2,1)} %bitcast.2) | data formatting | bytes 12582912 | tf_op jit(solution)/shard_map/reshape | solution.py:12
  314.2 47.8 %all-to-all-done = bf16[16,32,4096]{2,1,0:T(8,128)(2,1)} async-done(((bf16[16,32,4096]{2,1,0:T(8,128)(2,1)}), bf16[16,32,4096]{2,1,0:T(8,128)(2,1)}, u32[]{:S(2)}, u32[]{:S(2)}) %all-to-all-start) | async-done | bytes 4194336 | tf_op jit(solution)/shard_map/all_to_all | solution.py:36
  362.0 0.0 copy-start.4
  362.0 7.0 %convolution_bitcast_fusion = f32[3,512,256]{2,1,0:T(8,128)S(1)} fusion(bf16[512,4096,1]{1,0,2:T(8,128)(2,1)} %bitcast.1, bf16[3,4096,256]{2,1,0:T(8,128)(2,1)} %bitcast.34), kind=kOutput, calls=%fused_computation | convolution fusion | flops 3221225472 | bytes 12058624 | tf_op jit(solution)/shard_map/sk,ikc->isc/dot_general | solution.py:39
  369.1 0.1 fusion.24
  369.2 1.5 fusion.10
  370.6 0.0 copy-done.4
  370.6 1.2 fusion
  371.9 19.9 %all_to_all.21 = f32[16,1,16]{2,1,0:T(1,128)S(1)} all-to-all(f32[16,1,16]{2,1,0:T(1,128)S(1)} %broadcast_in_dim.8), channel_id=1, replica_groups=mesh['fsdp'=32,'tp'=16] {'tp'}, dimensions={0} | all-to-all | bytes 2048 | tf_op jit(solution)/shard_map/all_to_all | solution.py:53
  391.8 4.0 all-to-all-start.2
  395.8 0.5 multiply_bitcast_fusion
  396.4 8.2 %all-to-all-done.2 = bf16[16,32,256]{2,1,0:T(8,128)(2,1)S(1)} async-done(((bf16[16,32,256]{2,1,0:T(8,128)(2,1)}), bf16[16,32,256]{2,1,0:T(8,128)(2,1)S(1)}, u32[]{:S(2)}, u32[]{:S(2)}) %all-to-all-start.2) | async-done | bytes 262176 | tf_op jit(solution)/shard_map/all_to_all | solution.py:58
  404.6 0.7 copy.19
  (4 shorter events, 0.0 us)
Async XLA Ops:
  5.0 17.2 %copy-start = (bf16[32,4096]{1,0:T(8,128)(2,1)S(1)}, bf16[32,4096]{1,0:T(8,128)(2,1)}, u32[]{:S(2)}) copy-start(bf16[32,4096]{1,0:T(8,128)(2,1)} %param.7) | copy-start | bytes 786436
  5.0 17.4 %copy-start.1 = (f32[4096]{0:T(1024)S(1)}, f32[4096]{0:T(1024)}, u32[]{:S(2)}) copy-start(f32[4096]{0:T(1024)} %param.8) | copy-start | bytes 49156
  5.0 290.9 %all-to-all-start.1 = ((bf16[32,3,128,256]{3,2,1,0:T(8,128)(2,1)}), bf16[32,3,128,256]{3,2,1,0:T(8,128)(2,1)}, u32[]{:S(2)}, u32[]{:S(2)}) async-start(bf16[32,3,128,256]{3,2,1,0:T(8,128)(2,1)} %stack.2), calls=%async_computation.1 | async-start | bytes 12582912 | tf_op jit(solution)/shard_map/all_to_all | solution.py:12
  298.3 8.6 %copy-start.2 = (f32[16,7]{0,1:T(8,128)S(1)}, f32[16,7]{0,1:T(8,128)}, u32[]{:S(2)}) copy-start(f32[16,7]{0,1:T(8,128)} %param.10) | copy-start | bytes 1348
  298.3 9.6 %copy-start.3 = (s32[1,512]{1,0:T(1,128)S(1)}, s32[1,512]{1,0:T(1,128)}, u32[]{:S(2)}) copy-start(s32[1,512]{1,0:T(1,128)} %param.11) | copy-start | bytes 6148
  298.3 63.7 %all-to-all-start = ((bf16[16,32,4096]{2,1,0:T(8,128)(2,1)}), bf16[16,32,4096]{2,1,0:T(8,128)(2,1)}, u32[]{:S(2)}, u32[]{:S(2)}) async-start(bf16[16,32,4096]{2,1,0:T(8,128)(2,1)} %broadcast_in_dim.6), calls=%async_computation | async-start | bytes 8388608 | tf_op jit(solution)/shard_map/all_to_all | solution.py:36
  362.0 8.6 %copy-start.4 = (s32[1,16]{1,0:T(1,128)S(1)}, s32[1,16]{1,0:T(1,128)}, u32[]{:S(2)}) copy-start(s32[1,16]{1,0:T(1,128)} %param.12) | copy-start | bytes 196
  391.8 12.7 %all-to-all-start.2 = ((bf16[16,32,256]{2,1,0:T(8,128)(2,1)}), bf16[16,32,256]{2,1,0:T(8,128)(2,1)S(1)}, u32[]{:S(2)}, u32[]{:S(2)}) async-start(bf16[16,32,256]{2,1,0:T(8,128)(2,1)} %bitcast.15), calls=%async_computation.2 | async-start | bytes 524288 | tf_op jit(solution)/shard_map/all_to_all | solution.py:58
